TPU v7x, 256 devices: a whole 4x4x8 slice. The times are simulated.
256 devices in a mesh: seq: 64 (over x, z, core), head: 4 (over y).
Axes of the slice: x: 4, y: 4, z: 8, core: 2. Of those that a mesh axis runs over, the one named last changes fastest.
Arguments:
- queries: bfloat16 [65536, 2048], P('seq', 'head'), may hold values from -48 to 48
- keys: bfloat16 [65536, 2048], P('seq', 'head'), may hold values from -48 to 48
- values: bfloat16 [65536, 2048], P('seq', 'head'), may hold values from -6 to 6
- memory_keys: bfloat16 [65536, 2048], P('seq', 'head'), may hold values from -48 to 48
- memory_values: bfloat16 [65536, 2048], P('seq', 'head'), may hold values from -6 to 6
- block_ids: int32 [512, 4], P('seq'), may hold values from 0 to 1023, as said below
- gate_bias: float32 [16], P('head'), may hold values from -2 to 2
- out_weight: bfloat16 [2048, 2048], P('head'), may hold values from -0.5 to 0.5
Outputs:
- layer_out: bfloat16 [65536, 2048], P(('seq', 'head'))
Inputs may be any that keep to these rules, and one draw needn't show every extreme that they name: `block_ids`: block b belongs to owner b // 16. Among the 8 x 4 ids of one device's rows no id repeats; exactly 2 of them name blocks of owner 64 - 1, block 1023 always among them, and no other owner is named more than 1 times.
All inputs are finite; a program needn't handle non-finite values.
Results may differ from a plain program's by a relative error of at most 0.013.
Values may be sent and summed in bfloat16 or wider, within the bound.
No kernel may reach another device: no remote copies, remote signals or barrier semaphores. Data moves between devices by JAX's collectives and lax.ppermute only.
A program may use at most 192 MiB of HBM per device.

v0:
```python
import math
import jax
import jax.numpy as jnp
from jax import lax
from jax.sharding import PartitionSpec as P

HDIM = 128
WINDOW = 1024
QBLK = 128
MROWS = 64
TOPM = 4
NEG_FILL = -1e30


def passed_along(value, axis, steps):
    count = lax.axis_size(axis)
    leading, last = (max(0, -steps), min(count, count - steps))
    return lax.ppermute(value, axis, [(source, source + steps) for source in range(leading, last)])


def masked_softmax(scores, allowed):
    row_max = jnp.max(jnp.where(allowed, scores, NEG_FILL), axis=-1, keepdims=True)
    weights = jnp.where(allowed, jnp.exp(scores - row_max), 0.0)
    return (weights / jnp.sum(weights, axis=-1, keepdims=True)).astype(jnp.bfloat16)


def window_attention(queries, ext_keys, ext_values, first_row):
    tok_rows, features = queries.shape
    heads_here = features // HDIM
    tile_rows = math.gcd(tok_rows, 512)
    key_span = tile_rows + WINDOW
    score_scale = 1.0 / math.sqrt(HDIM)

    def per_tile(step_index):
        row_start = step_index * tile_rows
        query_tile = lax.dynamic_slice_in_dim(queries, row_start, tile_rows, 0).reshape(
            tile_rows, heads_here, HDIM
        )
        key_tile = lax.dynamic_slice_in_dim(ext_keys, row_start, key_span, 0).reshape(
            key_span, heads_here, HDIM
        )
        value_tile = lax.dynamic_slice_in_dim(ext_values, row_start, key_span, 0).reshape(
            key_span, heads_here, HDIM
        )
        scores = (
            jnp.einsum("qhd,khd->hqk", query_tile, key_tile, preferred_element_type=jnp.float32)
            * score_scale
        )
        query_pos = first_row + row_start + jnp.arange(tile_rows, dtype=jnp.int32)
        key_pos = first_row + row_start - WINDOW + jnp.arange(key_span, dtype=jnp.int32)
        allowed = (
            (key_pos[None, :] <= query_pos[:, None])
            & (key_pos[None, :] > query_pos[:, None] - WINDOW)
            & (key_pos[None, :] >= 0)
        )
        attend_weights = masked_softmax(scores, allowed[None])
        return jnp.einsum(
            "hqk,khd->qhd", attend_weights, value_tile, preferred_element_type=jnp.float32
        )

    return lax.map(per_tile, jnp.arange(tok_rows // tile_rows, dtype=jnp.int32)).reshape(
        tok_rows, heads_here, HDIM
    )


def memory_attention(queries, fetched):
    tok_rows, features = queries.shape
    heads_here = features // HDIM
    block_count = tok_rows // QBLK
    score_scale = 1.0 / math.sqrt(HDIM)
    query_blocks = queries.reshape(block_count, QBLK, heads_here, HDIM)
    key_blocks = fetched[:, 0].reshape(block_count, TOPM * MROWS, heads_here, HDIM)
    value_blocks = fetched[:, 1].reshape(block_count, TOPM * MROWS, heads_here, HDIM)
    scores = (
        jnp.einsum("bqhd,bkhd->bhqk", query_blocks, key_blocks, preferred_element_type=jnp.float32)
        * score_scale
    )
    attend_weights = masked_softmax(scores, jnp.ones(scores.shape, dtype=bool))
    remote = jnp.einsum(
        "bhqk,bkhd->bqhd", attend_weights, value_blocks, preferred_element_type=jnp.float32
    )
    return remote.reshape(tok_rows, heads_here, HDIM)


def build_table(slot_index, offset, in_use, total_slots):
    matches = (jnp.arange(total_slots, dtype=jnp.int32)[:, None] == slot_index[None, :]) & in_use[
        None, :
    ]
    return jnp.sum(jnp.where(matches, offset[None, :] + 1, 0), axis=1) - 1


def on_device(queries, keys, values, memory_keys, memory_values, block_ids, gate_bias, out_weight):
    tok_rows, features = queries.shape
    owners = lax.axis_size("seq")
    groups = lax.axis_size("head")
    seq_index = lax.axis_index("seq")
    first_row = seq_index * tok_rows
    full_weight = lax.all_gather(out_weight, "head", axis=0, tiled=True)
    request_count = block_ids.shape[0] * block_ids.shape[1]
    wanted = block_ids.reshape(request_count)
    mem_dev = memory_keys.shape[0] // MROWS
    last_block = owners * mem_dev - 1
    owner_index = wanted // mem_dev
    offset = wanted % mem_dev
    is_last = wanted == last_block
    memory_store = jnp.stack(
        (
            memory_keys.reshape(mem_dev, MROWS, features),
            memory_values.reshape(mem_dev, MROWS, features),
        ),
        axis=1,
    )
    edge_rows = jnp.stack((keys, values))
    before = passed_along(edge_rows, "seq", 1)
    shared = lax.psum(
        jnp.where(
            seq_index == owners - 1, memory_store[mem_dev - 1], jnp.zeros_like(memory_store[0])
        ),
        "seq",
    )
    every_id = lax.all_gather(block_ids, "seq", axis=0, tiled=True).reshape(owners, request_count)
    mine = (every_id // mem_dev == seq_index) & (every_id != last_block)
    asked_for = jnp.sum(jnp.where(mine, every_id % mem_dev + 1, 0), axis=1) - 1
    outgoing = memory_store[jnp.maximum(asked_for, 0)]
    before, outgoing, shared = lax.optimization_barrier((before, outgoing, shared))
    returned = lax.all_to_all(outgoing, "seq", split_axis=0, concat_axis=0, tiled=True)
    local_part = window_attention(
        queries, jnp.concatenate([before[0], keys]), jnp.concatenate([before[1], values]), first_row
    )
    fetched = jnp.where(is_last[:, None, None, None], shared[None], returned[owner_index])
    remote = memory_attention(queries, fetched)
    mixing = jax.nn.sigmoid(gate_bias)[None, :, None]
    attended = (
        (mixing * remote + (1.0 - mixing) * local_part)
        .reshape(tok_rows, features)
        .astype(jnp.bfloat16)
    )
    out_rows = tok_rows // groups
    gathered = lax.all_to_all(
        attended.reshape(groups, out_rows, features),
        "head",
        split_axis=0,
        concat_axis=0,
        tiled=True,
    )
    partials = jnp.einsum(
        "gqf,gfn->gqn",
        gathered,
        full_weight.reshape(groups, features, full_weight.shape[1]),
        preferred_element_type=jnp.float32,
    ).astype(jnp.bfloat16)
    return jnp.sum(partials.astype(jnp.float32), axis=0).astype(jnp.bfloat16)


def solution(mesh):
    in_specs = (
        P("seq", "head"),
        P("seq", "head"),
        P("seq", "head"),
        P("seq", "head"),
        P("seq", "head"),
        P("seq", None),
        P("head"),
        P("head", None),
    )
    out_specs = P(("seq", "head"), None)
    return jax.shard_map(
        on_device, mesh=mesh, in_specs=in_specs, out_specs=out_specs, check_vma=False
    )
```

profile of v0, /device:TPU:1, one launch (start us, length us, event | category | flops | bytes accessed | tf_op | source)
XLA Modules:
  0.0 452.9 jit_solution(179319438945823830)
XLA Ops:
  7.4 1.6 copy.52
  11.2 5.0 %collective-permute-start = (bf16[2,1024,512]{1,2,0:T(8,128)(2,1)}, bf16[2,1024,512]{1,2,0:T(8,128)(2,1)}, u32[]{:S(2)}, u32[]{:S(2)}) collective-permute-start(bf16[2,1024,512]{1,2,0:T(8,128)(2,1)} %pad_maximum_fusion.1), channel_id=1, source_target_pairs={{0,4},{4,8},{8,12},{12,16},{16,20},{20,24},{24,28},{28,32},{32,36}... | collective-permute-start | bytes 6291464 | tf_op jit(solution)/shard_map/ppermute | solution.py:18
  17.8 62.6 %all-gather = s32[64,8,4]{1,2,0:T(4,128)S(1)} all-gather(s32[1,8,4]{1,2,0:T(4,128)S(1)} %bitcast.85), channel_id=1, replica_groups=mesh['seq'=64,'head'=4] {'seq'}, dimensions={0}, use_global_device_ids=true | all-gather | bytes 8320 | tf_op jit(solution)/shard_map/all_gather | solution.py:121
  80.7 1.7 pad_maximum_fusion
  82.5 5.5 %gather_fusion = bf16[64,2,64,512]{3,2,1,0:T(8,128)(2,1)} fusion(bf16[16,2,64,512]{3,2,1,0:T(8,128)(2,1)S(1)} %pad_maximum_fusion, s32[1024]{0:T(1024)S(1)} %pad_clamp_fusion.1), kind=kCustom, calls=%fused_computation | custom fusion | bytes 16777472 | tf_op jit(solution)/shard_map/gather | solution.py:124
  88.0 108.2 %all-reduce.2.cloned.1.call-done = bf16[2,64,512]{2,1,0:T(8,128)(2,1)} async-done(((bf16[2,64,512]{2,1,0:T(8,128)(2,1)}), bf16[2,64,512]{2,1,0:T(8,128)(2,1)}) %all-reduce.2.cloned.1.call-update) | async-done | bytes 131088 | tf_op jit(solution)/shard_map/psum | solution.py:115
  196.2 6.7 %all-to-all-start = ((bf16[64,2,64,512]{3,2,1,0:T(8,128)(2,1)}), bf16[64,2,64,512]{3,2,1,0:T(8,128)(2,1)}, u32[]{:S(2)}, u32[]{:S(2)}) async-start(bf16[64,2,64,512]{3,2,1,0:T(8,128)(2,1)} %gather_fusion), calls=%async_computation | async-start | bytes 16777216 | tf_op jit(solution)/shard_map/all_to_all | solution.py:126
  205.9 1.8 slice_bitcast_fusion
  207.8 1.7 pad_maximum_fusion.2
  209.4 60.5 %while.13 = (s32[]{:T(128)}, f32[2,512,4,128]{3,2,1,0:T(4,128)}, s32[2]{0:T(128)S(1)}, bf16[2048,512]{0,1:T(8,128)(2,1)S(1)}, s32[]{:T(128)}, /*index=5*/bf16[10...) while((s32[]{:T(128)}, f32[2,512,4,128]{3,2,1,0:T(4,128)}, ...), condition=%wide.region_8.9_spmd, body=%wide.region_5.8_spmd.sunk | while | flops 2444237824 | bytes 44080892 | solution.py:61
  211.5 3.3 constant_dynamic-slice_fusion.5
  216.9 11.6 %fusion.59 = (f32[4,512]{1,0:T(4,128)S(1)}, f32[4,512,1536]{2,1,0:T(8,128)}) fusion(pred[512,1536]{1,0:T(8,128)(4,1)S(1)} %and_and_fusion.2, bf16[512,4,128]{0,2,1:T(8,128)(2,1)} %bitcast.78, bf16[1536,4,128]{0,2,1:T(8,128)(2,1)} %bitcast.77), kind=kOutput, calls=%fused_computation.78.clone.1 | convolution fusion | flops 1629488640 | bytes 15474688 | tf_op jit(solution)/shard_map/while/body/eval_jaxpr/sub | solution.py:23
  228.5 8.5 %fusion.60 = f32[1,512,4,128]{1,3,2,0:T(8,128)} fusion(bf16[1536,4,128]{0,2,1:T(8,128)(2,1)} %bitcast.76, f32[4,512,1536]{2,1,0:T(8,128)} %get-tuple-element.234, f32[4,512]{1,0:T(4,128)S(1)} %get-tuple-element.235), kind=kOutput, calls=%fused_computation.14.clone.1 | convolution fusion | flops 811597824 | bytes 15212544 | tf_op jit(solution)/shard_map/while/body/eval_jaxpr/hqk,khd->qhd/dot_general | solution.py:57
  237.0 1.6 copy.85
  241.8 3.4 constant_dynamic-slice_fusion.5
  247.2 11.6 %fusion.59 = (f32[4,512]{1,0:T(4,128)S(1)}, f32[4,512,1536]{2,1,0:T(8,128)}) fusion(pred[512,1536]{1,0:T(8,128)(4,1)S(1)} %and_and_fusion.2, bf16[512,4,128]{0,2,1:T(8,128)(2,1)} %bitcast.78, bf16[1536,4,128]{0,2,1:T(8,128)(2,1)} %bitcast.77), kind=kOutput, calls=%fused_computation.78.clone.1 | convolution fusion | flops 1629488640 | bytes 15474688 | tf_op jit(solution)/shard_map/while/body/eval_jaxpr/sub | solution.py:23
  258.8 8.4 %fusion.60 = f32[1,512,4,128]{1,3,2,0:T(8,128)} fusion(bf16[1536,4,128]{0,2,1:T(8,128)(2,1)} %bitcast.76, f32[4,512,1536]{2,1,0:T(8,128)} %get-tuple-element.234, f32[4,512]{1,0:T(4,128)S(1)} %get-tuple-element.235), kind=kOutput, calls=%fused_computation.14.clone.1 | convolution fusion | flops 811597824 | bytes 15212544 | tf_op jit(solution)/shard_map/while/body/eval_jaxpr/hqk,khd->qhd/dot_general | solution.py:57
  267.3 1.6 copy.85
  269.9 3.1 reshape.263
  273.1 115.5 %all-to-all-done = bf16[64,2,64,512]{3,2,1,0:T(8,128)(2,1)} async-done(((bf16[64,2,64,512]{3,2,1,0:T(8,128)(2,1)}), bf16[64,2,64,512]{3,2,1,0:T(8,128)(2,1)}, u32[]{:S(2)}, u32[]{:S(2)}) %all-to-all-start) | async-done | bytes 8388640 | tf_op jit(solution)/shard_map/all_to_all | solution.py:126
  388.6 6.2 %gather_fusion.1 = bf16[32,2,64,512]{3,2,1,0:T(8,128)(2,1)} fusion(bf16[64,2,64,512]{3,2,1,0:T(8,128)(2,1)} %all-to-all-done, s32[1024]{0:T(1024)S(1)} %pad_clamp_fusion), kind=kCustom, calls=%fused_computation.1 | custom fusion | bytes 8388736 | tf_op jit(solution)/shard_map/gather | solution.py:130
  394.8 2.6 broadcast_select_fusion
  397.3 2.3 fusion.38
  399.6 2.5 reshape_squeeze.7
  402.2 4.1 reshape_squeeze.6
  407.0 3.1 fusion.39
  411.0 1.8 copy.62
  412.9 3.2 reshape.262
  416.1 3.1 add_convert_fusion
  419.2 4.0 all-to-all-start.1
  423.2 15.3 %all-to-all-done.1 = bf16[4,256,512]{2,1,0:T(8,128)(2,1)S(1)} async-done(((bf16[4,256,512]{2,1,0:T(8,128)(2,1)}), bf16[4,256,512]{2,1,0:T(8,128)(2,1)S(1)}, u32[]{:S(2)}, u32[]{:S(2)}) %all-to-all-start.1) | async-done | bytes 1048608 | tf_op jit(solution)/shard_map/all_to_all | solution.py:139
  438.5 6.9 %convert_reduce_fusion = bf16[256,2048]{1,0:T(8,128)(2,1)} fusion(bf16[4,256,512]{2,1,0:T(8,128)(2,1)S(1)} %all-to-all-done.1, bf16[4,512,2048]{2,1,0:T(8,128)(2,1)} %bitcast.86), kind=kOutput, calls=%fused_computation.30 | convolution fusion | flops 2151153664 | bytes 10485760 | tf_op jit(solution)/shard_map/gqf,gfn->gqn/dot_general | solution.py:146
  (72 shorter events, 17.8 us)
Async XLA Ops:
  7.4 1.6 copy-start.7
  7.4 188.8 %all-reduce.2.cloned.1.call-start = ((), (), s32[]{:S(2)}) async-start(), calls=%async_computation.2 | async-start | bytes 262144 | tf_op jit(solution)/shard_map/psum | solution.py:115
  9.5 1.7 copy-start.1
  9.5 6.7 %copy-start.5 = (bf16[1024,512]{1,0:T(8,128)(2,1)S(1)}, bf16[1024,512]{1,0:T(8,128)(2,1)}, u32[]{:S(2)}) copy-start(bf16[1024,512]{1,0:T(8,128)(2,1)} %param.14) | copy-start | bytes 3145732
  11.2 6.6 %copy-start.9 = (s32[8,4]{0,1:T(4,128)S(1)}, s32[8,4]{0,1:T(4,128)}, u32[]{:S(2)}) copy-start(s32[8,4]{0,1:T(4,128)} %param.15) | copy-start | bytes 388
  11.2 185.0 %collective-permute-start = (bf16[2,1024,512]{1,2,0:T(8,128)(2,1)}, bf16[2,1024,512]{1,2,0:T(8,128)(2,1)}, u32[]{:S(2)}, u32[]{:S(2)}) collective-permute-start(bf16[2,1024,512]{1,2,0:T(8,128)(2,1)} %pad_maximum_fusion.1), channel_id=1, source_target_pairs={{0,4},{4,8},{8,12},{12,16},{16,20},{20,24},{24,28},{28,32},{32,36}... | collective-permute-start | bytes 6291464 | tf_op jit(solution)/shard_map/ppermute | solution.py:18
  196.2 192.4 %all-to-all-start = ((bf16[64,2,64,512]{3,2,1,0:T(8,128)(2,1)}), bf16[64,2,64,512]{3,2,1,0:T(8,128)(2,1)}, u32[]{:S(2)}, u32[]{:S(2)}) async-start(bf16[64,2,64,512]{3,2,1,0:T(8,128)(2,1)} %gather_fusion), calls=%async_computation | async-start | bytes 16777216 | tf_op jit(solution)/shard_map/all_to_all | solution.py:126
  202.9 1.2 copy-start
  202.9 2.3 copy-start.12
  202.9 220.3 %all-gather.3.cloned.1.call-start = ((), (), s32[]{:S(2)}) async-start(), calls=%async_computation.3 | async-start | bytes 10485760 | tf_op jit(solution)/shard_map/all_gather | solution.py:98
  205.9 1.9 copy-start.2
  273.1 121.7 %copy-start.8 = (bf16[2,64,512]{2,1,0:T(8,128)(2,1)S(1)}, bf16[2,64,512]{2,1,0:T(8,128)(2,1)}, u32[]{:S(2)}) copy-start(bf16[2,64,512]{2,1,0:T(8,128)(2,1)} %all-reduce.2.cloned.1.call-done) | copy-start | bytes 393220
  402.2 4.1 copy-start.4
  407.0 3.1 copy-start.6
  412.9 3.2 copy-start.3
  412.9 3.2 copy-start.10
  412.9 3.2 copy-start.11
  419.2 19.3 %all-to-all-start.1 = ((bf16[4,256,512]{2,1,0:T(8,128)(2,1)}), bf16[4,256,512]{2,1,0:T(8,128)(2,1)S(1)}, u32[]{:S(2)}, u32[]{:S(2)}) async-start(bf16[4,256,512]{2,1,0:T(8,128)(2,1)} %add_convert_fusion), calls=%async_computation.1 | async-start | bytes 2097152 | tf_op jit(solution)/shard_map/all_to_all | solution.py:139
Sparse Core Ops, SparseCore 0:
  17.9 178.2 all-reduce.1
Sparse Core Ops, SparseCore 1:
  205.2 86.2 all-gather.2
where the time goes:
time: 454 us; the launch traced here: 453 us
  waiting for transfers between devices  239 us (53%)
  blocking collectives  62.6 us (14%)
  local copies, waits for them, and re-layouts  52.9 us (12%)
  matrix products  48.6 us (11%)
  other arithmetic  17 us (4%)
  starting transfers between devices  15.9 us (4%)
  between operations  15.1 us (3%)
    all_to_all x1, waiting for transfers between devices, on_device(): lax.all_to_all(outgoing, 'seq', split_axis=0, concat_axis=0, tiled=True)  116 us
    psum x1, waiting for transfers between devices, on_device(): lax.psum(jnp.where(seq_index == owners - 1, memory_store[mem_dev - 1], jn...  108 us
    all_gather x1, blocking collectives, on_device(): lax.all_gather(block_ids, 'seq', axis=0, tiled=True)  62.6 us
    sub x2, matrix products, masked_softmax(): weights = jnp.where(allowed, jnp.exp(scores - row_max), 0.0)  23.2 us
    dot_general x2, matrix products, per_tile(): jnp.einsum('hqk,khd->qhd', attend_weights, value_tile, preferred_element_...  16.9 us
    all_to_all x1, waiting for transfers between devices, on_device(): lax.all_to_all(attended.reshape(groups, out_rows, features), 'head', spli...  15.3 us
  transfers between devices with their start and end apart: 5, of which 3 were waited for; matrix products, arithmetic and copies ran while one was open for 24% of the time, Pallas kernels for 0%

commit v1 on v0

--- a/solution.py
+++ b/solution.py
@@ -112,11 +112,14 @@
     )
     edge_rows = jnp.stack((keys, values))
     before = passed_along(edge_rows, "seq", 1)
-    shared = lax.psum(
-        jnp.where(
-            seq_index == owners - 1, memory_store[mem_dev - 1], jnp.zeros_like(memory_store[0])
+    shared = jnp.sum(
+        lax.all_gather(
+            jnp.where(
+                seq_index == owners - 1, memory_store[mem_dev - 1], jnp.zeros_like(memory_store[0])
+            ),
+            "seq",
         ),
-        "seq",
+        axis=0,
     )
     every_id = lax.all_gather(block_ids, "seq", axis=0, tiled=True).reshape(owners, request_count)
     mine = (every_id // mem_dev == seq_index) & (every_id != last_block)

time: 454 us -> 360 us (0.79)
  waiting for transfers between devices: 239 us -> 136 us
  blocking collectives: 62.6 us -> 68.8 us
  other arithmetic: 17 us -> 21.9 us
    psum x1 -> x0, waiting for transfers between devices: 108 us -> none  [on_device(): lax.psum(jnp.where(seq_index == owners - 1, memory_store[mem_dev - 1], jn...]
    all_gather x1, blocking collectives: 62.6 us -> 68.8 us  [on_device(): lax.all_gather(block_ids, 'seq', axis=0, tiled=True)]
    all_gather x0 -> x1, waiting for transfers between devices: none -> 5.15 us  [on_device(): lax.all_gather(jnp.where(seq_index == owners - 1, memory_store[mem_dev -...]
    reduce_sum x0 -> x1, other arithmetic: none -> 4.54 us  [on_device(): jnp.sum(lax.all_gather(jnp.where(seq_index == owners - 1, memory_store[me...]
  transfers between devices with their start and end apart: 5 -> 5, of which waited for: 3 -> 3; matrix products, arithmetic and copies ran while one was open for 24% -> 32% of each run, Pallas kernels for 0% -> 0%
where the time goes in v1:
time: 360 us; the launch traced here: 359 us
  waiting for transfers between devices  136 us (38%)
  blocking collectives  68.8 us (19%)
  local copies, waits for them, and re-layouts  51.8 us (14%)
  matrix products  48.6 us (14%)
  other arithmetic  21.9 us (6%)
  starting transfers between devices  15.2 us (4%)
  between operations  15.1 us (4%)
    all_to_all x1, waiting for transfers between devices, on_device(): lax.all_to_all(outgoing, 'seq', split_axis=0, concat_axis=0, tiled=True)  116 us
    all_gather x1, blocking collectives, on_device(): lax.all_gather(block_ids, 'seq', axis=0, tiled=True)  68.8 us
    sub x2, matrix products, masked_softmax(): weights = jnp.where(allowed, jnp.exp(scores - row_max), 0.0)  23.2 us
    dot_general x2, matrix products, per_tile(): jnp.einsum('hqk,khd->qhd', attend_weights, value_tile, preferred_element_...  16.9 us
    all_to_all x1, waiting for transfers between devices, on_device(): lax.all_to_all(attended.reshape(groups, out_rows, features), 'head', spli...  15.3 us
  transfers between devices with their start and end apart: 5, of which 3 were waited for; matrix products, arithmetic and copies ran while one was open for 32% of the time, Pallas kernels for 0%

profile of v1, /device:TPU:1, one launch (start us, length us, event | category | flops | bytes accessed | tf_op | source)
XLA Modules:
  0.0 359.2 jit_solution(15208147572421947657)
XLA Ops:
  7.4 1.7 fusion.30
  10.2 1.7 pad_maximum_fusion.1
  11.9 4.9 %collective-permute-start = (bf16[2,1024,512]{1,2,0:T(8,128)(2,1)}, bf16[2,1024,512]{1,2,0:T(8,128)(2,1)}, u32[]{:S(2)}, u32[]{:S(2)}) collective-permute-start(bf16[2,1024,512]{1,2,0:T(8,128)(2,1)} %pad_maximum_fusion.1), channel_id=1, source_target_pairs={{0,4},{4,8},{8,12},{12,16},{16,20},{20,24},{24,28},{28,32},{32,36}... | collective-permute-start | bytes 6291464 | tf_op jit(solution)/shard_map/ppermute | solution.py:18
  16.8 68.8 %all-gather = s32[64,8,4]{1,2,0:T(4,128)S(1)} all-gather(s32[1,8,4]{1,2,0:T(4,128)S(1)} %bitcast.79), channel_id=1, replica_groups=mesh['seq'=64,'head'=4] {'seq'}, dimensions={0}, use_global_device_ids=true | all-gather | bytes 8320 | tf_op jit(solution)/shard_map/all_gather | solution.py:124
  86.0 1.8 pad_maximum_fusion
  87.8 5.6 %gather_fusion = bf16[64,2,64,512]{3,2,1,0:T(8,128)(2,1)} fusion(bf16[16,2,64,512]{3,2,0,1:T(8,128)(2,1)S(1)} %pad_maximum_fusion, s32[1024]{0:T(1024)S(1)} %pad_clamp_fusion.1), kind=kCustom, calls=%fused_computation | custom fusion | bytes 16777472 | tf_op jit(solution)/shard_map/gather | solution.py:127
  93.3 5.1 %all-gather.4.cloned.1.call-done = bf16[64,2,64,512]{3,2,0,1:T(8,128)(2,1)} async-done(((bf16[1,2,64,512]{3,2,0,1:T(8,128)(2,1)}), bf16[64,2,64,512]{3,2,0,1:T(8,128)(2,1)}) %all-gather.4.cloned.1.call-update) | async-done | bytes 8388624 | tf_op jit(solution)/shard_map/all_gather | solution.py:116
  98.5 4.5 %reduce_sum.65 = bf16[2,64,512]{2,1,0:T(8,128)(2,1)S(1)} reduce(bf16[64,2,64,512]{3,2,0,1:T(8,128)(2,1)} %all-gather.4.cloned.1.call-done, bf16[]{:T(256)} %constant.139.clone.1), dimensions={0}, to_apply=%region_2.3 | reduce | flops 4128768 | bytes 8519682 | tf_op jit(solution)/shard_map/reduce_sum | solution.py:115
  103.0 6.1 %all-to-all-start = ((bf16[64,2,64,512]{3,2,1,0:T(8,128)(2,1)}), bf16[64,2,64,512]{3,2,1,0:T(8,128)(2,1)}, u32[]{:S(2)}, u32[]{:S(2)}) async-start(bf16[64,2,64,512]{3,2,1,0:T(8,128)(2,1)} %gather_fusion), calls=%async_computation | async-start | bytes 16777216 | tf_op jit(solution)/shard_map/all_to_all | solution.py:129
  112.1 1.8 slice_bitcast_fusion
  114.0 1.6 pad_maximum_fusion.2
  115.6 60.5 %while.13 = (s32[]{:T(128)}, f32[2,512,4,128]{3,2,1,0:T(4,128)}, s32[2]{0:T(128)S(1)}, bf16[2048,512]{0,1:T(8,128)(2,1)S(1)}, s32[]{:T(128)}, /*index=5*/bf16[10...) while((s32[]{:T(128)}, f32[2,512,4,128]{3,2,1,0:T(4,128)}, ...), condition=%wide.region_8.9_spmd, body=%wide.region_5.8_spmd.sunk | while | flops 2444237824 | bytes 44080892 | solution.py:61
  117.7 3.3 constant_dynamic-slice_fusion.5
  123.1 11.6 %fusion.60 = (f32[4,512]{1,0:T(4,128)S(1)}, f32[4,512,1536]{2,1,0:T(8,128)}) fusion(pred[512,1536]{1,0:T(8,128)(4,1)S(1)} %and_and_fusion.2, bf16[512,4,128]{0,2,1:T(8,128)(2,1)} %bitcast.72, bf16[1536,4,128]{0,2,1:T(8,128)(2,1)} %bitcast.71), kind=kOutput, calls=%fused_computation.78.clone.1 | convolution fusion | flops 1629488640 | bytes 15474688 | tf_op jit(solution)/shard_map/while/body/eval_jaxpr/sub | solution.py:23
  134.7 8.5 %fusion.61 = f32[1,512,4,128]{1,3,2,0:T(8,128)} fusion(bf16[1536,4,128]{0,2,1:T(8,128)(2,1)} %bitcast.70, f32[4,512,1536]{2,1,0:T(8,128)} %get-tuple-element.234, f32[4,512]{1,0:T(4,128)S(1)} %get-tuple-element.235), kind=kOutput, calls=%fused_computation.14.clone.1 | convolution fusion | flops 811597824 | bytes 15212544 | tf_op jit(solution)/shard_map/while/body/eval_jaxpr/hqk,khd->qhd/dot_general | solution.py:57
  148.0 3.4 constant_dynamic-slice_fusion.5
  153.4 11.6 %fusion.60 = (f32[4,512]{1,0:T(4,128)S(1)}, f32[4,512,1536]{2,1,0:T(8,128)}) fusion(pred[512,1536]{1,0:T(8,128)(4,1)S(1)} %and_and_fusion.2, bf16[512,4,128]{0,2,1:T(8,128)(2,1)} %bitcast.72, bf16[1536,4,128]{0,2,1:T(8,128)(2,1)} %bitcast.71), kind=kOutput, calls=%fused_computation.78.clone.1 | convolution fusion | flops 1629488640 | bytes 15474688 | tf_op jit(solution)/shard_map/while/body/eval_jaxpr/sub | solution.py:23
  165.0 8.4 %fusion.61 = f32[1,512,4,128]{1,3,2,0:T(8,128)} fusion(bf16[1536,4,128]{0,2,1:T(8,128)(2,1)} %bitcast.70, f32[4,512,1536]{2,1,0:T(8,128)} %get-tuple-element.234, f32[4,512]{1,0:T(4,128)S(1)} %get-tuple-element.235), kind=kOutput, calls=%fused_computation.14.clone.1 | convolution fusion | flops 811597824 | bytes 15212544 | tf_op jit(solution)/shard_map/while/body/eval_jaxpr/hqk,khd->qhd/dot_general | solution.py:57
  176.1 3.1 reshape.260
  179.3 115.6 %all-to-all-done = bf16[64,2,64,512]{3,2,1,0:T(8,128)(2,1)} async-done(((bf16[64,2,64,512]{3,2,1,0:T(8,128)(2,1)}), bf16[64,2,64,512]{3,2,1,0:T(8,128)(2,1)}, u32[]{:S(2)}, u32[]{:S(2)}) %all-to-all-start) | async-done | bytes 8388640 | tf_op jit(solution)/shard_map/all_to_all | solution.py:129
  294.8 6.2 %gather_fusion.1 = bf16[32,2,64,512]{3,2,1,0:T(8,128)(2,1)} fusion(bf16[64,2,64,512]{3,2,1,0:T(8,128)(2,1)} %all-to-all-done, s32[1024]{0:T(1024)S(1)} %pad_clamp_fusion), kind=kCustom, calls=%fused_computation.1 | custom fusion | bytes 8388736 | tf_op jit(solution)/shard_map/gather | solution.py:133
  301.0 2.6 broadcast_select_fusion
  303.6 2.3 fusion.39
  305.9 2.5 reshape_squeeze.7
  308.4 4.0 %reshape_squeeze.6 = bf16[8,256,4,128]{3,2,1,0:T(4,128)(2,1)} reshape(bf16[32,1,64,512]{3,2,1,0:T(8,128)(2,1)} %get-tuple-element.171) | data formatting | bytes 4194304 | tf_op jit(solution)/shard_map/reshape;squeeze | solution.py:73
  313.2 3.1 fusion.40
  317.2 1.8 copy.58
  319.1 3.2 reshape.259
  322.3 3.1 add_convert_fusion
  325.4 4.0 %all-to-all-start.1 = ((bf16[4,256,512]{2,1,0:T(8,128)(2,1)}), bf16[4,256,512]{2,1,0:T(8,128)(2,1)S(1)}, u32[]{:S(2)}, u32[]{:S(2)}) async-start(bf16[4,256,512]{2,1,0:T(8,128)(2,1)} %add_convert_fusion), calls=%async_computation.1 | async-start | bytes 2097152 | tf_op jit(solution)/shard_map/all_to_all | solution.py:142
  329.4 15.3 %all-to-all-done.1 = bf16[4,256,512]{2,1,0:T(8,128)(2,1)S(1)} async-done(((bf16[4,256,512]{2,1,0:T(8,128)(2,1)}), bf16[4,256,512]{2,1,0:T(8,128)(2,1)S(1)}, u32[]{:S(2)}, u32[]{:S(2)}) %all-to-all-start.1) | async-done | bytes 1048608 | tf_op jit(solution)/shard_map/all_to_all | solution.py:142
  344.8 6.9 %convert_reduce_fusion = bf16[256,2048]{1,0:T(8,128)(2,1)} fusion(bf16[4,256,512]{2,1,0:T(8,128)(2,1)S(1)} %all-to-all-done.1, bf16[4,512,2048]{2,1,0:T(8,128)(2,1)} %bitcast.80), kind=kOutput, calls=%fused_computation.30 | convolution fusion | flops 2151153664 | bytes 10485760 | tf_op jit(solution)/shard_map/gqf,gfn->gqn/dot_general | solution.py:149
  (71 shorter events, 18.4 us)
Async XLA Ops:
  7.4 1.7 copy-start.6
  7.4 91.1 %all-gather.4.cloned.1.call-start = ((), (), s32[]{:S(2)}) async-start(), calls=%async_computation.2 | async-start | bytes 8519680 | tf_op jit(solution)/shard_map/all_gather | solution.py:116
  7.4 2.3 copy-start.7
  10.2 1.7 copy-start.1
  10.2 6.6 %copy-start.8 = (s32[8,4]{0,1:T(4,128)S(1)}, s32[8,4]{0,1:T(4,128)}, u32[]{:S(2)}) copy-start(s32[8,4]{0,1:T(4,128)} %param.15) | copy-start | bytes 388
  11.9 91.2 %collective-permute-start = (bf16[2,1024,512]{1,2,0:T(8,128)(2,1)}, bf16[2,1024,512]{1,2,0:T(8,128)(2,1)}, u32[]{:S(2)}, u32[]{:S(2)}) collective-permute-start(bf16[2,1024,512]{1,2,0:T(8,128)(2,1)} %pad_maximum_fusion.1), channel_id=1, source_target_pairs={{0,4},{4,8},{8,12},{12,16},{16,20},{20,24},{24,28},{28,32},{32,36}... | collective-permute-start | bytes 6291464 | tf_op jit(solution)/shard_map/ppermute | solution.py:18
  103.0 191.8 %all-to-all-start = ((bf16[64,2,64,512]{3,2,1,0:T(8,128)(2,1)}), bf16[64,2,64,512]{3,2,1,0:T(8,128)(2,1)}, u32[]{:S(2)}, u32[]{:S(2)}) async-start(bf16[64,2,64,512]{3,2,1,0:T(8,128)(2,1)} %gather_fusion), calls=%async_computation | async-start | bytes 16777216 | tf_op jit(solution)/shard_map/all_to_all | solution.py:129
  109.1 1.2 copy-start
  109.1 2.3 copy-start.11
  109.1 220.3 %all-gather.6.cloned.1.call-start = ((), (), s32[]{:S(2)}) async-start(), calls=%async_computation.3 | async-start | bytes 10485760 | tf_op jit(solution)/shard_map/all_gather | solution.py:98
  112.1 1.9 copy-start.2
  308.4 4.1 %copy-start.4 = (bf16[8,128,4,128]{3,2,1,0:T(4,128)(2,1)S(1)}, bf16[8,128,4,128]{3,2,1,0:T(4,128)(2,1)}, u32[]{:S(2)}) copy-start(bf16[8,128,4,128]{3,2,1,0:T(4,128)(2,1)} %reshape.258) | copy-start | bytes 3145732
  313.2 3.1 copy-start.5
  319.1 3.2 copy-start.3
  319.1 3.2 copy-start.9
  319.1 3.2 copy-start.10
  325.4 19.4 %all-to-all-start.1 = ((bf16[4,256,512]{2,1,0:T(8,128)(2,1)}), bf16[4,256,512]{2,1,0:T(8,128)(2,1)S(1)}, u32[]{:S(2)}, u32[]{:S(2)}) async-start(bf16[4,256,512]{2,1,0:T(8,128)(2,1)} %add_convert_fusion), calls=%async_computation.1 | async-start | bytes 2097152 | tf_op jit(solution)/shard_map/all_to_all | solution.py:142
Sparse Core Ops, SparseCore 0:
  11.0 87.4 all-gather.3
Sparse Core Ops, SparseCore 1:
  111.4 86.2 all-gather.5
